TPU v7x, 512 devices: a whole 4x8x8 slice. The times are simulated.
512 devices in a mesh: seq: 64 (over x, z, core), kvh: 4 (over y_hi), rep: 2 (over y_lo).
Axes of the slice: x: 4, y: 8 (y_hi: 4, y_lo: 2; y = y_hi * 2 + y_lo), z: 8, core: 2. Of those that a mesh axis runs over, the one named last changes fastest.
Arguments:
- vision_states: bfloat16 [64, 384, 1152], P('seq', 'kvh'), may hold values from -24 to 24
- frame_tokens: int32 [64], replicated, may hold values from 128 to 384, as said below
- norm_gain: float32 [1152], replicated, may hold values from 0.1 to 1.9
- projector: bfloat16 [1152, 3584], P(None, ('kvh', 'rep')), may hold values from -0.1875 to 0.1875
- head_weights: bfloat16 [3584, 3072], P(('kvh', 'rep')), may hold values from -4 to 4
Outputs:
- attended: bfloat16 [256, 64, 2048], P(None, 'seq', ('kvh', 'rep'))
Inputs may be any that keep to these rules, and one draw needn't show every extreme that they name: `frame_tokens`: the counts sum to 16384, and some frame has exactly 384 tokens.
All inputs are finite; a program needn't handle non-finite values.
Results may differ from a plain program's by a relative error of at most 0.0062.
Values may be sent and summed in bfloat16 or wider, within the bound.
No kernel may reach another device: no remote copies, remote signals or barrier semaphores. Data moves between devices by JAX's collectives and lax.ppermute only.
A program may use at most 128 MiB of HBM per device.

v0:
```python
import jax
import jax.numpy as jnp
from jax import lax
from jax.sharding import PartitionSpec as P

KV_HEADS = 4
HEAD_DIM = 128
GROUP_HEADS = 4
norm_eps = 1e-06
masked_score = -1e30


def layer_norm(states, norm_gain):
    values = states.astype(jnp.float32)
    center = values - jnp.mean(values, axis=-1, keepdims=True)
    spread = jnp.mean(center * center, axis=-1, keepdims=True)
    return (center * lax.rsqrt(spread + norm_eps) * norm_gain).astype(jnp.bfloat16)


def attention_step(queries, query_pos, key_rows, key_base, seq_count):
    scale = queries.shape[-1] ** (-0.5)

    def add_keys(carry, piece, start):
        context, top, total = carry
        key_piece, value_piece = piece
        number = key_piece.shape[0]
        index = jnp.arange(number, dtype=jnp.int32)
        key_pos = (key_base + index % key_rows) * seq_count + index // key_rows
        allowed = (key_pos[None, :] <= query_pos[:, None])[:, None, :]
        scores = (
            jnp.einsum("qhd,kd->qhk", queries, key_piece, preferred_element_type=jnp.float32)
            * scale
        )
        scores = jnp.where(allowed, scores, masked_score)
        new_top = jnp.maximum(top, jnp.max(scores, axis=-1))
        weights = jnp.where(allowed, jnp.exp(scores - new_top[..., None]), 0.0)
        total = jnp.sum(weights, axis=-1)
        update = jnp.einsum(
            "qhk,kd->qhd",
            weights.astype(jnp.bfloat16),
            value_piece,
            preferred_element_type=jnp.float32,
        )
        return (update, new_top, total)

    return add_keys


def empty_partials(tok_rows, head_count):
    return (
        jnp.zeros((tok_rows, head_count, HEAD_DIM), jnp.float32),
        jnp.full((tok_rows, head_count), masked_score, jnp.float32),
        jnp.zeros((tok_rows, head_count), jnp.float32),
    )


def local(vision_states, frame_tokens, norm_gain, projector, head_weights):
    seq_count = lax.axis_size("seq")
    seq_index = lax.axis_index("seq")
    rep_count = lax.axis_size("rep")
    frames_dev = vision_states.shape[0]
    frame_max = vision_states.shape[1] * lax.axis_size("kvh")
    d_cols = projector.shape[1]
    cap_frame = frame_max // seq_count
    tok_rows = 2 * frames_dev * frame_max // 3
    heads_local = GROUP_HEADS // rep_count
    normed = layer_norm(vision_states, norm_gain)
    hidden = jnp.einsum(
        "frv,vc->frc",
        lax.all_gather(normed, "kvh", axis=1, tiled=True),
        projector,
        preferred_element_type=jnp.float32,
    )
    visual_frames = jax.nn.gelu(hidden, approximate=False).astype(jnp.bfloat16)
    ends = jnp.cumsum(frame_tokens)
    starts_all = ends - frame_tokens
    my_starts = lax.dynamic_slice_in_dim(starts_all, seq_index * frames_dev, frames_dev, 0)
    dest = jnp.arange(seq_count, dtype=jnp.int32)[:, None, None]
    slots = jnp.arange(cap_frame, dtype=jnp.int32)[None, None, :]
    frame_local = jnp.arange(frames_dev, dtype=jnp.int32)[None, :, None]
    row_of = jnp.mod(dest - my_starts[None, :, None], seq_count) + slots * seq_count
    send_index = (frame_local * frame_max + row_of).reshape(-1)
    outgoing = visual_frames.reshape(frames_dev * frame_max, d_cols)[send_index]
    received = lax.all_to_all(outgoing, "seq", split_axis=0, concat_axis=0, tiled=True)
    query_pos = jnp.arange(tok_rows, dtype=jnp.int32) * seq_count + seq_index
    before = ends[None, :] <= query_pos[:, None]
    frame = jnp.sum(before.astype(jnp.int32), axis=1)
    offset = jnp.sum(jnp.where(before, frame_tokens[None, :], 0), axis=1)
    slot_index = frame * cap_frame + (query_pos - offset) // seq_count
    visual = received[slot_index]
    wide = head_weights.reshape(d_cols, KV_HEADS, GROUP_HEADS + 2, HEAD_DIM)
    query_w = wide[:, :, :GROUP_HEADS].reshape(d_cols, KV_HEADS, rep_count, heads_local * HEAD_DIM)
    pair_w = wide[:, :, GROUP_HEADS:].reshape(d_cols, KV_HEADS, 1, 2 * HEAD_DIM)
    pair_w = jnp.broadcast_to(pair_w, (d_cols, KV_HEADS, rep_count, 2 * HEAD_DIM))
    piece_w = jnp.concatenate([query_w, pair_w], axis=3).reshape(
        d_cols, KV_HEADS * rep_count, (heads_local + 2) * HEAD_DIM
    )
    summed = lax.psum_scatter(
        jnp.einsum("tc,cpw->ptw", visual, piece_w, preferred_element_type=jnp.float32),
        ("kvh", "rep"),
        scatter_dimension=0,
        tiled=True,
    )[0]
    head_rows = summed.astype(jnp.bfloat16)
    queries = head_rows[:, : heads_local * HEAD_DIM].reshape(tok_rows, heads_local, HEAD_DIM)
    key_own = head_rows[:, heads_local * HEAD_DIM : (heads_local + 1) * HEAD_DIM]
    value_own = head_rows[:, (heads_local + 1) * HEAD_DIM :]
    add_keys = attention_step(queries, query_pos, tok_rows, 0, seq_count)
    context, top, total = add_keys(
        empty_partials(tok_rows, heads_local),
        (
            lax.all_gather(key_own, "seq", axis=0, tiled=True),
            lax.all_gather(value_own, "seq", axis=0, tiled=True),
        ),
        jnp.int32(0),
    )
    result = (context / total[..., None]).astype(jnp.bfloat16)
    return result.reshape(tok_rows, 1, heads_local * HEAD_DIM)


def solution(mesh):
    placed = (P("seq", "kvh", None), P(), P(), P(None, ("kvh", "rep")), P(("kvh", "rep"), None))
    return jax.shard_map(
        local, mesh=mesh, in_specs=placed, out_specs=P(None, "seq", ("kvh", "rep")), check_vma=False
    )
```

profile of v0, /device:TPU:1, one launch (start us, length us, event | category | flops | bytes accessed | tf_op | source)
XLA Modules:
  0.0 328.2 jit_solution(847766380383886331)
XLA Ops:
  9.7 1.1 convert_reduce_fusion
  10.8 1.2 fusion.42
  12.0 1.1 fusion.44
  13.1 22.0 %all_gather.9 = bf16[1,384,1152]{2,1,0:T(8,128)(2,1)S(1)} all-gather(bf16[1,96,1152]{2,1,0:T(8,128)(2,1)S(1)} %fusion.44), channel_id=1, replica_groups=mesh['seq'=64,'kvh'=4,'rep'=2] {'kvh'}, dimensions={1}, use_global_device_ids=true | all-gather | bytes 1105920 | tf_op jit(solution)/shard_map/all_gather | solution.py:70
  35.2 2.1 fusion.30
  37.5 2.1 gather_fusion
  39.5 1.0 all_to_all.8
  40.5 16.4 %all-to-all-start = ((bf16[64,6,448]{2,1,0:T(8,128)(2,1)}), bf16[64,6,448]{2,1,0:T(8,128)(2,1)S(1)}, u32[]{:S(2)}, u32[]{:S(2)}) async-start(bf16[64,6,448]{2,1,0:T(8,128)(2,1)} %all_to_all.8), calls=%async_computation | async-start | bytes 1048576 | tf_op jit(solution)/shard_map/all_to_all | solution.py:84
  57.1 4.6 %copy.23 = bf16[448,3072]{0,1:T(8,128)(2,1)} copy(bf16[448,3072]{1,0:T(8,128)(2,1)} %param.9) | data formatting | bytes 5505024 | tf_op args[4]
  61.6 1.8 slice.24
  63.4 2.3 slice.25
  65.7 2.3 copy.26
  68.1 1.5 copy.25
  69.7 4.6 %all-to-all-done = bf16[64,6,448]{2,1,0:T(8,128)(2,1)S(1)} async-done(((bf16[64,6,448]{2,1,0:T(8,128)(2,1)}), bf16[64,6,448]{2,1,0:T(8,128)(2,1)S(1)}, u32[]{:S(2)}, u32[]{:S(2)}) %all-to-all-start) | async-done | bytes 344096 | tf_op jit(solution)/shard_map/all_to_all | solution.py:84
  74.5 1.2 gather_fusion.1
  75.8 4.8 %fusion.13 = f32[8,256,512]{1,2,0:T(8,128)} fusion(bf16[448,8,256]{2,0,1:T(8,128)(2,1)S(1)} %bitcast.45, bf16[448,8,256]{2,0,1:T(8,128)(2,1)} %copy.26, bf16[256,448]{1,0:T(8,128)(2,1)S(1)} %gather_fusion.1), kind=kOutput, calls=%fused_computation.17 | convolution fusion | flops 946864128 | bytes 8093696 | tf_op jit(solution)/shard_map/tc,cpw->ptw/dot_general | solution.py:99
  80.7 51.4 %reduce-scatter.2.cloned.1.call-done = f32[1,256,512]{1,2,0:T(8,128)} async-done(((f32[8,256,512]{1,2,0:T(8,128)}), f32[1,256,512]{1,2,0:T(8,128)}) %reduce-scatter.2.cloned.1.call-update) | async-done | bytes 524304 | tf_op jit(solution)/shard_map/reduce_scatter | solution.py:98
  132.1 1.1 convert_bitcast_fusion
  134.6 4.3 %broadcast_compare_fusion = pred[256,16384]{1,0:T(8,128)(4,1)} fusion(s32[16384]{0:T(1024)S(1)} %fusion.54, s32[256]{0:T(256)S(1)} %multiply_add_fusion), kind=kLoop, calls=%fused_computation.9 | loop fusion | flops 4194304 | bytes 4260864 | tf_op jit(solution)/shard_map/le | solution.py:29
  138.9 78.7 %all-gather.3.cloned.1.call-done = bf16[16384,128]{0,1:T(8,128)(2,1)} async-done(((bf16[256,128]{0,1:T(8,128)(2,1)}), bf16[16384,128]{0,1:T(8,128)(2,1)}) %all-gather.3.cloned.1.call-update) | async-done | bytes 4194320 | tf_op jit(solution)/shard_map/all_gather | solution.py:112
  217.6 17.6 %fusion = (f32[256,2]{0,1:T(2,128)S(1)}, f32[256,2,16384]{2,0,1:T(8,128)}) fusion(pred[256,16384]{1,0:T(8,128)(4,1)} %broadcast_compare_fusion, bf16[256,2,128]{0,2,1:T(8,128)(2,1)S(1)} %bitcast.46, bf16[16384,128]{0,1:T(8,128)(2,1)} %all-gather.3.cloned.1.call-done), kind=kOutput, calls=%fused_computation.4 | convolution fusion | flops 2172648960 | bytes 42076160 | tf_op jit(solution)/shard_map/qhd,kd->qhk/dot_general | solution.py:31
  235.2 16.3 %fusion.1 = f32[256,2]{0,1:T(2,128)S(1)} fusion(f32[256,2,16384]{2,0,1:T(8,128)} %get-tuple-element.10, f32[256,2]{0,1:T(2,128)S(1)} %broadcast_maximum_fusion, pred[256,16384]{1,0:T(8,128)(4,1)} %broadcast_compare_fusion), kind=kLoop, calls=%fused_computation.5 | loop fusion | flops 41942528 | bytes 37752832 | tf_op jit(solution)/shard_map/reduce_sum | solution.py:37
  251.5 50.8 %all-gather.5.cloned.1.call-done = bf16[16384,128]{0,1:T(8,128)(2,1)} async-done(((bf16[256,128]{0,1:T(8,128)(2,1)}), bf16[16384,128]{0,1:T(8,128)(2,1)}) %all-gather.5.cloned.1.call-update) | async-done | bytes 4194320 | tf_op jit(solution)/shard_map/all_gather | solution.py:113
  302.3 18.5 %fusion.21 = bf16[256,2,128]{0,2,1:T(8,128)(2,1)S(1)} fusion(bf16[16384,128]{0,1:T(8,128)(2,1)} %all-gather.5.cloned.1.call-done, f32[256,2,16384]{2,0,1:T(8,128)} %get-tuple-element.10, f32[256,2]{0,1:T(2,128)S(1)} %broadcast_maximum_fusion, pred[256,16384]{1,0:T(8,128)(4,1)} %broadcast_compare_fusion, f32[256,2]{0,1:T(2,128)S(1)} %fusion.1), kind=kOutput, calls=%fused_computation.19 | convolution fusion | flops 2189557760 | bytes 42078208 | tf_op jit(solution)/shard_map/qhk,kd->qhd/dot_general | solution.py:38
  (38 shorter events, 6.2 us)
Async XLA Ops:
  6.5 28.6 %copy-start = (bf16[1152,448]{0,1:T(8,128)(2,1)S(1)}, bf16[1152,448]{0,1:T(8,128)(2,1)}, u32[]{:S(2)}) copy-start(bf16[1152,448]{0,1:T(8,128)(2,1)} %param.8) | copy-start | bytes 3096580
  40.5 33.8 %all-to-all-start = ((bf16[64,6,448]{2,1,0:T(8,128)(2,1)}), bf16[64,6,448]{2,1,0:T(8,128)(2,1)S(1)}, u32[]{:S(2)}, u32[]{:S(2)}) async-start(bf16[64,6,448]{2,1,0:T(8,128)(2,1)} %all_to_all.8), calls=%async_computation | async-start | bytes 1048576 | tf_op jit(solution)/shard_map/all_to_all | solution.py:84
  57.0 75.1 %reduce-scatter.2.cloned.1.call-start = ((), (), s32[]{:S(2)}) async-start(), calls=%async_computation.2 | async-start | bytes 4718592 | tf_op jit(solution)/shard_map/reduce_scatter | solution.py:98
  57.0 12.5 %copy-start.2 = (s32[64]{0:T(128)S(1)}, s32[64]{0:T(128)}, u32[]{:S(2)}) copy-start(s32[64]{0:T(128)} %param.6) | copy-start | bytes 772
  80.6 137.0 %all-gather.3.cloned.1.call-start = ((), (), s32[]{:S(2)}) async-start(), calls=%async_computation.3 | async-start | bytes 4259840 | tf_op jit(solution)/shard_map/all_gather | solution.py:112
  133.8 168.5 %all-gather.5.cloned.1.call-start = ((), (), s32[]{:S(2)}) async-start(), calls=%async_computation.4 | async-start | bytes 4259840 | tf_op jit(solution)/shard_map/all_gather | solution.py:113
  302.3 19.3 %copy-start.1 = (bf16[1152,448]{0,1:T(8,128)(2,1)S(1)}, bf16[1152,448]{0,1:T(8,128)(2,1)}, u32[]{:S(2)}) copy-start(bf16[1152,448]{0,1:T(8,128)(2,1)} %param.8) | copy-start | bytes 3096580
Sparse Core Ops, SparseCore 0:
  80.7 51.2 reduce-scatter.1
  135.2 82.3 all-gather.2
  220.7 81.5 all-gather.4
where the time goes:
time: 329 us; the launch traced here: 328 us
  waiting for transfers between devices  186 us (57%)
  matrix products  43 us (13%)
  other arithmetic  26.9 us (8%)
  blocking collectives  22 us (7%)
  local copies, waits for them, and re-layouts  20.2 us (6%)
  starting transfers between devices  16.6 us (5%)
  between operations  13.3 us (4%)
    all_gather x1, waiting for transfers between devices, local(): lax.all_gather(key_own, 'seq', axis=0, tiled=True)  78.7 us
    reduce_scatter x1, waiting for transfers between devices, local(): lax.psum_scatter(jnp.einsum('tc,cpw->ptw', visual, piece_w, preferred_ele...  51.4 us
    all_gather x1, waiting for transfers between devices, local(): lax.all_gather(value_own, 'seq', axis=0, tiled=True)  50.8 us
    all_gather x1, blocking collectives, local(): lax.all_gather(normed, 'kvh', axis=1, tiled=True)  22 us
    dot_general x1, matrix products, add_keys(): jnp.einsum('qhk,kd->qhd', weights.astype(jnp.bfloat16), value_piece, pref...  18.5 us
    dot_general x1, matrix products, add_keys(): jnp.einsum('qhd,kd->qhk', queries, key_piece, preferred_element_type=jnp....  17.6 us
    all_to_all x1, starting transfers between devices, local(): lax.all_to_all(outgoing, 'seq', split_axis=0, concat_axis=0, tiled=True)  16.4 us
    reduce_sum x1, other arithmetic, add_keys(): total = jnp.sum(weights, axis=-1)  16.3 us
  transfers between devices with their start and end apart: 4, of which 4 were waited for; matrix products, arithmetic and copies ran while one was open for 15% of the time, Pallas kernels for 0%

commit v1 on v0

--- a/solution.py
+++ b/solution.py
@@ -67,7 +67,9 @@
     normed = layer_norm(vision_states, norm_gain)
     hidden = jnp.einsum(
         "frv,vc->frc",
-        lax.all_gather(normed, "kvh", axis=1, tiled=True),
+        jnp.concatenate(
+            lax.all_to_all(jnp.stack([normed] * lax.axis_size("kvh")), "kvh", 0, 0), axis=1
+        ),
         projector,
         preferred_element_type=jnp.float32,
     )

time: 329 us -> 333 us (1.012)
  blocking collectives: 22 us -> 0 us
  waiting for transfers between devices: 186 us -> 206 us
  starting transfers between devices: 16.6 us -> 21.9 us
    all_gather x1 -> x0, blocking collectives: 22 us -> none  [local(): lax.all_gather(normed, 'kvh', axis=1, tiled=True)]
    all_to_all x0 -> x1, waiting for transfers between devices: none -> 19.3 us  [local(): lax.all_to_all(jnp.stack([normed] * lax.axis_size('kvh')), 'kvh', 0, 0)]
    all_to_all x0 -> x1, starting transfers between devices: none -> 7.64 us  [local(): lax.all_to_all(jnp.stack([normed] * lax.axis_size('kvh')), 'kvh', 0, 0)]
  transfers between devices with their start and end apart: 4 -> 5, of which waited for: 4 -> 5; matrix products, arithmetic and copies ran while one was open for 15% -> 16% of each run, Pallas kernels for 0% -> 0%
where the time goes in v1:
time: 333 us
  waiting for transfers between devices  206 us (62%)
  matrix products  43 us (13%)
  other arithmetic  26.9 us (8%)
  starting transfers between devices  21.9 us (7%)
  local copies, waits for them, and re-layouts  21.1 us (6%)
  between operations  13.3 us (4%)
    all_gather x1, waiting for transfers between devices, local(): lax.all_gather(key_own, 'seq', axis=0, tiled=True)  78.7 us
    reduce_scatter x1, waiting for transfers between devices, local(): lax.psum_scatter(jnp.einsum('tc,cpw->ptw', visual, piece_w, preferred_ele...  52.4 us
    all_gather x1, waiting for transfers between devices, local(): lax.all_gather(value_own, 'seq', axis=0, tiled=True)  50.8 us
    all_to_all x1, waiting for transfers between devices, local(): lax.all_to_all(jnp.stack([normed] * lax.axis_size('kvh')), 'kvh', 0, 0)  19.3 us
    dot_general x1, matrix products, add_keys(): jnp.einsum('qhk,kd->qhd', weights.astype(jnp.bfloat16), value_piece, pref...  18.5 us
    dot_general x1, matrix products, add_keys(): jnp.einsum('qhd,kd->qhk', queries, key_piece, preferred_element_type=jnp....  17.6 us
    reduce_sum x1, other arithmetic, add_keys(): total = jnp.sum(weights, axis=-1)  16.3 us
    all_to_all x1, starting transfers between devices, local(): lax.all_to_all(outgoing, 'seq', split_axis=0, concat_axis=0, tiled=True)  14.1 us
  transfers between devices with their start and end apart: 5, of which 5 were waited for; matrix products, arithmetic and copies ran while one was open for 16% of the time, Pallas kernels for 0%

profile of v1, /device:TPU:1, one launch (start us, length us, event | category | flops | bytes accessed | tf_op | source)
XLA Modules:
  0.0 332.8 jit_solution(6692738283900959432)
XLA Ops:
  6.5 1.1 convert_reduce_fusion
  7.7 1.2 fusion.38
  8.9 1.1 fusion.42
  11.0 7.6 %all-to-all-start = ((bf16[4,1,96,1152]{3,2,1,0:T(8,128)(2,1)}), bf16[4,1,96,1152]{3,2,1,0:T(8,128)(2,1)S(1)}, u32[]{:S(2)}, u32[]{:S(2)}) async-start(bf16[4,1,96,1152]{3,2,1,0:T(8,128)(2,1)} %stack.2), calls=%async_computation | async-start | bytes 1769472 | tf_op jit(solution)/shard_map/all_to_all | solution.py:71
  21.8 19.3 %all-to-all-done = bf16[4,1,96,1152]{3,2,1,0:T(8,128)(2,1)S(1)} async-done(((bf16[4,1,96,1152]{3,2,1,0:T(8,128)(2,1)}), bf16[4,1,96,1152]{3,2,1,0:T(8,128)(2,1)S(1)}, u32[]{:S(2)}, u32[]{:S(2)}) %all-to-all-start) | async-done | bytes 884768 | tf_op jit(solution)/shard_map/all_to_all | solution.py:71
  41.0 2.1 fusion.28
  43.3 2.1 gather_fusion
  46.4 14.1 %all-to-all-start.1 = ((bf16[64,6,448]{2,1,0:T(8,128)(2,1)}), bf16[64,6,448]{2,1,0:T(8,128)(2,1)S(1)}, u32[]{:S(2)}, u32[]{:S(2)}) async-start(bf16[64,6,448]{2,1,0:T(8,128)(2,1)} %all_to_all.12), calls=%async_computation.1 | async-start | bytes 1048576 | tf_op jit(solution)/shard_map/all_to_all | solution.py:86
  60.6 4.6 %copy.23 = bf16[448,3072]{0,1:T(8,128)(2,1)} copy(bf16[448,3072]{1,0:T(8,128)(2,1)} %param.9) | data formatting | bytes 5505024 | tf_op args[4]
  65.2 1.8 slice.24
  67.0 2.3 slice.25
  69.3 2.3 copy.26
  71.6 1.5 copy.25
  73.3 4.6 %all-to-all-done.1 = bf16[64,6,448]{2,1,0:T(8,128)(2,1)S(1)} async-done(((bf16[64,6,448]{2,1,0:T(8,128)(2,1)}), bf16[64,6,448]{2,1,0:T(8,128)(2,1)S(1)}, u32[]{:S(2)}, u32[]{:S(2)}) %all-to-all-start.1) | async-done | bytes 344096 | tf_op jit(solution)/shard_map/all_to_all | solution.py:86
  78.1 1.2 gather_fusion.1
  79.4 4.8 %fusion.13 = f32[8,256,512]{1,2,0:T(8,128)} fusion(bf16[448,8,256]{2,0,1:T(8,128)(2,1)S(1)} %bitcast.44, bf16[448,8,256]{2,0,1:T(8,128)(2,1)} %copy.26, bf16[256,448]{1,0:T(8,128)(2,1)S(1)} %gather_fusion.1), kind=kOutput, calls=%fused_computation.17 | convolution fusion | flops 946864128 | bytes 8093696 | tf_op jit(solution)/shard_map/tc,cpw->ptw/dot_general | solution.py:101
  84.2 52.4 %reduce-scatter.2.cloned.1.call-done = f32[1,256,512]{1,2,0:T(8,128)} async-done(((f32[8,256,512]{1,2,0:T(8,128)}), f32[1,256,512]{1,2,0:T(8,128)}) %reduce-scatter.2.cloned.1.call-update) | async-done | bytes 524304 | tf_op jit(solution)/shard_map/reduce_scatter | solution.py:100
  136.6 1.1 convert_bitcast_fusion
  139.1 4.3 %broadcast_compare_fusion = pred[256,16384]{1,0:T(8,128)(4,1)} fusion(s32[16384]{0:T(1024)S(1)} %fusion.51, s32[256]{0:T(256)S(1)} %multiply_add_fusion), kind=kLoop, calls=%fused_computation.9 | loop fusion | flops 4194304 | bytes 4260864 | tf_op jit(solution)/shard_map/le | solution.py:29
  143.5 78.7 %all-gather.3.cloned.1.call-done = bf16[16384,128]{0,1:T(8,128)(2,1)} async-done(((bf16[256,128]{0,1:T(8,128)(2,1)}), bf16[16384,128]{0,1:T(8,128)(2,1)}) %all-gather.3.cloned.1.call-update) | async-done | bytes 4194320 | tf_op jit(solution)/shard_map/all_gather | solution.py:114
  222.2 17.6 %fusion = (f32[256,2]{0,1:T(2,128)S(1)}, f32[256,2,16384]{2,0,1:T(8,128)}) fusion(pred[256,16384]{1,0:T(8,128)(4,1)} %broadcast_compare_fusion, bf16[256,2,128]{0,2,1:T(8,128)(2,1)S(1)} %bitcast.46, bf16[16384,128]{0,1:T(8,128)(2,1)} %all-gather.3.cloned.1.call-done), kind=kOutput, calls=%fused_computation.4 | convolution fusion | flops 2172648960 | bytes 42076160 | tf_op jit(solution)/shard_map/qhd,kd->qhk/dot_general | solution.py:31
  239.8 16.3 %fusion.1 = f32[256,2]{0,1:T(2,128)S(1)} fusion(f32[256,2,16384]{2,0,1:T(8,128)} %get-tuple-element.10, f32[256,2]{0,1:T(2,128)S(1)} %broadcast_maximum_fusion, pred[256,16384]{1,0:T(8,128)(4,1)} %broadcast_compare_fusion), kind=kLoop, calls=%fused_computation.5 | loop fusion | flops 41942528 | bytes 37752832 | tf_op jit(solution)/shard_map/reduce_sum | solution.py:37
  256.1 50.8 %all-gather.5.cloned.1.call-done = bf16[16384,128]{0,1:T(8,128)(2,1)} async-done(((bf16[256,128]{0,1:T(8,128)(2,1)}), bf16[16384,128]{0,1:T(8,128)(2,1)}) %all-gather.5.cloned.1.call-update) | async-done | bytes 4194320 | tf_op jit(solution)/shard_map/all_gather | solution.py:115
  306.9 18.5 %fusion.21 = bf16[256,2,128]{0,2,1:T(8,128)(2,1)S(1)} fusion(bf16[16384,128]{0,1:T(8,128)(2,1)} %all-gather.5.cloned.1.call-done, f32[256,2,16384]{2,0,1:T(8,128)} %get-tuple-element.10, f32[256,2]{0,1:T(2,128)S(1)} %broadcast_maximum_fusion, pred[256,16384]{1,0:T(8,128)(4,1)} %broadcast_compare_fusion, f32[256,2]{0,1:T(2,128)S(1)} %fusion.1), kind=kOutput, calls=%fused_computation.19 | convolution fusion | flops 2189557760 | bytes 42078208 | tf_op jit(solution)/shard_map/qhk,kd->qhd/dot_general | solution.py:38
  (40 shorter events, 8.0 us)
Async XLA Ops:
  6.5 34.5 %copy-start = (bf16[1152,448]{0,1:T(8,128)(2,1)S(1)}, bf16[1152,448]{0,1:T(8,128)(2,1)}, u32[]{:S(2)}) copy-start(bf16[1152,448]{0,1:T(8,128)(2,1)} %param.8) | copy-start | bytes 3096580
  11.0 30.0 %all-to-all-start = ((bf16[4,1,96,1152]{3,2,1,0:T(8,128)(2,1)}), bf16[4,1,96,1152]{3,2,1,0:T(8,128)(2,1)S(1)}, u32[]{:S(2)}, u32[]{:S(2)}) async-start(bf16[4,1,96,1152]{3,2,1,0:T(8,128)(2,1)} %stack.2), calls=%async_computation | async-start | bytes 1769472 | tf_op jit(solution)/shard_map/all_to_all | solution.py:71
  46.4 31.5 %all-to-all-start.1 = ((bf16[64,6,448]{2,1,0:T(8,128)(2,1)}), bf16[64,6,448]{2,1,0:T(8,128)(2,1)S(1)}, u32[]{:S(2)}, u32[]{:S(2)}) async-start(bf16[64,6,448]{2,1,0:T(8,128)(2,1)} %all_to_all.12), calls=%async_computation.1 | async-start | bytes 1048576 | tf_op jit(solution)/shard_map/all_to_all | solution.py:86
  60.5 76.1 %reduce-scatter.2.cloned.1.call-start = ((), (), s32[]{:S(2)}) async-start(), calls=%async_computation.3 | async-start | bytes 4718592 | tf_op jit(solution)/shard_map/reduce_scatter | solution.py:100
  60.6 12.5 %copy-start.2 = (s32[64]{0:T(128)S(1)}, s32[64]{0:T(128)}, u32[]{:S(2)}) copy-start(s32[64]{0:T(128)} %param.6) | copy-start | bytes 772
  84.2 138.0 %all-gather.3.cloned.1.call-start = ((), (), s32[]{:S(2)}) async-start(), calls=%async_computation.4 | async-start | bytes 4259840 | tf_op jit(solution)/shard_map/all_gather | solution.py:114
  138.4 168.5 %all-gather.5.cloned.1.call-start = ((), (), s32[]{:S(2)}) async-start(), calls=%async_computation.5 | async-start | bytes 4259840 | tf_op jit(solution)/shard_map/all_gather | solution.py:115
  306.9 19.3 %copy-start.1 = (bf16[1152,448]{0,1:T(8,128)(2,1)S(1)}, bf16[1152,448]{0,1:T(8,128)(2,1)}, u32[]{:S(2)}) copy-start(bf16[1152,448]{0,1:T(8,128)(2,1)} %param.8) | copy-start | bytes 3096580
Sparse Core Ops, SparseCore 0:
  84.3 52.2 reduce-scatter.1
  139.8 82.3 all-gather.2
  225.3 81.5 all-gather.4
